TPU v7x, 256 devices: a whole 4x4x8 slice. The times are simulated.
256 devices in a mesh: gx: 64 (over z, y, core), gy: 4 (over x).
Axes of the slice: x: 4, y: 4, z: 8, core: 2. Of those that a mesh axis runs over, the one named last changes fastest.
Arguments:
- embeds: bfloat16 [256, 2048, 768], P('gx', 'gy'), may hold values from -6 to 6
- fetch_list: int32 [2, 64, 64], replicated, may hold values from 0 to 16383, as said below
- partners: int32 [2, 64, 64, 2], replicated, may hold values from 0 to 255, as said below
- counts: int32 [256], replicated, may hold values from 512 to 2048
Outputs:
- nearest: float32 [256, 2048], P('gx', 'gy')
Inputs may be any that keep to these rules, and one draw needn't show every extreme that they name: fetch_list[w, h, g] // 64 is a block stored by index g of gx, that is g * 4 <= fetch_list[w, h, g] // 64 < (g + 1) * 4. partners[w, h, g, :] are 2 different blocks stored by index h of gx, none equal to fetch_list[w, h, g] // 64.
All inputs are finite; a program needn't handle non-finite values.
Results may differ from a plain program's by a relative error of at most 0.0003.
Values may be sent and summed in bfloat16 or wider, within the bound.
No kernel may reach another device: no remote copies, remote signals or barrier semaphores. Data moves between devices by JAX's collectives and lax.ppermute only.
A program may use at most 192 MiB of HBM per device.

v0:
```python
import jax
import jax.numpy as jnp
from jax import lax
from jax.sharding import PartitionSpec as P

SLICE = 8
EPS = 1e-06


def normalize(source):
    values = source.astype(jnp.float32)
    return (values * lax.rsqrt(jnp.sum(values * values, axis=-1, keepdims=True) + EPS)).astype(
        jnp.bfloat16
    )


def dense_tiles(arrived, row_valid, chosen, owned_full, col_valid):
    slots, lent_rows, width = arrived.shape
    owned, block, _ = owned_full.shape
    flat_rows = arrived.reshape(slots * lent_rows, width)
    listed = jnp.any(
        chosen[:, :, None] == jnp.arange(owned, dtype=jnp.int32)[None, None, :], axis=1
    )
    listed_pairs = jnp.transpose(listed.reshape(slots, owned // 2, 2), (1, 0, 2))
    column_pairs = owned_full.reshape(owned // 2, 2, block, width)
    valid_pairs = col_valid.reshape(owned // 2, 2, block)

    def advance(best_rows, entries):
        columns, picked, valid_cols = entries
        scores = jnp.einsum("rd,cbd->rcb", flat_rows, columns, preferred_element_type=jnp.float32)
        scores = scores.reshape(slots, lent_rows, 2, block)
        keep = row_valid[:, :, None, None] & picked[:, None, :, None] & valid_cols[None, None, :, :]
        scores = jnp.where(keep, scores, jnp.float32(-1.0))
        return (jnp.maximum(best_rows, jnp.max(scores, axis=(2, 3))), jnp.max(scores, axis=(0, 1)))

    start = jnp.full((slots, lent_rows), -1.0, jnp.float32)
    best_rows, col_parts = lax.scan(advance, start, (column_pairs, listed_pairs, valid_pairs))
    return (best_rows, col_parts.reshape(owned, block))


def on_device(embeds, fetch_list, partners, counts):
    owned, quarter, width = embeds.shape
    slice_rows = SLICE
    pieces = quarter // slice_rows
    my_group = lax.axis_index("gx")
    my_lane = lax.axis_index("gy")
    block = quarter * lax.axis_size("gy")
    first = my_group * owned
    waves = fetch_list.shape[0]
    own_unit = normalize(embeds)
    own_pieces = own_unit.reshape(owned, pieces, slice_rows, width)
    owned_full = lax.all_gather(own_unit, "gy", axis=1, tiled=True)
    positions = jnp.arange(block, dtype=jnp.int32)
    own_counts = lax.dynamic_slice_in_dim(counts, first, owned)
    col_valid = positions[None, :] < own_counts[:, None]
    row_positions = my_lane * quarter + jnp.arange(quarter, dtype=jnp.int32)
    slice_offsets = my_lane * quarter + jnp.arange(slice_rows, dtype=jnp.int32)
    local_ids = jnp.arange(owned, dtype=jnp.int32)
    piece_ids = jnp.arange(pieces, dtype=jnp.int32)
    row_total = jnp.full((owned, quarter), -1.0, jnp.float32)
    col_total = jnp.full((owned, block), -1.0, jnp.float32)
    for wave_index in range(waves):
        tiles = lax.dynamic_index_in_dim(fetch_list[wave_index], my_group, 1, False)
        outgoing_sent_block = tiles // pieces - first
        outgoing_sent_piece = tiles % pieces
        outbound = own_pieces[outgoing_sent_block, outgoing_sent_piece]
        arrived = lax.all_to_all(outbound, "gx", split_axis=0, concat_axis=0, tiled=True)
        incoming = lax.dynamic_index_in_dim(fetch_list[wave_index], my_group, 0, False)
        arrived_counts = counts[incoming // pieces]
        arrived_rows = (incoming % pieces)[:, None] * slice_rows + slice_offsets[None, :]
        row_valid = arrived_rows < arrived_counts[:, None]
        chosen = lax.dynamic_index_in_dim(partners[wave_index], my_group, 0, False) - first
        row_best, col_best = dense_tiles(arrived, row_valid, chosen, owned_full, col_valid)
        returned = lax.all_to_all(row_best, "gx", split_axis=0, concat_axis=0, tiled=True)
        match = (outgoing_sent_block[:, None, None] == local_ids[None, :, None]) & (
            outgoing_sent_piece[:, None, None] == piece_ids[None, None, :]
        )
        placed = jnp.max(
            jnp.where(match[:, :, :, None], returned[:, None, None, :], jnp.float32(-1.0)), axis=0
        )
        row_total = jnp.maximum(row_total, placed.reshape(owned, quarter))
        col_total = jnp.maximum(col_total, col_best)
    col_all = lax.pmax(col_total, "gy")
    col_mine = lax.dynamic_slice_in_dim(col_all, my_lane * quarter, quarter, 1)
    nearest = jnp.maximum(row_total, col_mine)
    mine_valid = row_positions[None, :] < own_counts[:, None]
    return jnp.where(mine_valid, nearest, jnp.float32(-1.0))


def solution(mesh):
    in_specs = (P("gx", "gy", None), P(), P(), P())
    out_specs = P("gx", "gy")
    return jax.shard_map(
        on_device, mesh=mesh, in_specs=in_specs, out_specs=out_specs, check_vma=False
    )
```

profile of v0, /device:TPU:1, one launch (start us, length us, event | category | flops | bytes accessed | tf_op | source)
XLA Modules:
  0.0 224.2 jit_solution(3750707437659595756)
XLA Ops:
  6.5 2.7 %fusion.18 = f32[4,512]{1,0:T(4,128)S(1)} fusion(bf16[4,512,768]{2,1,0:T(8,128)(2,1)} %param.8), kind=kLoop, calls=%fused_computation.36 | loop fusion | flops 4716544 | bytes 3153920 | tf_op jit(solution)/shard_map/reduce_sum | solution.py:12
  9.3 4.1 %fusion.19 = bf16[4,512,768]{2,1,0:T(8,128)(2,1)} fusion(bf16[4,512,768]{2,1,0:T(8,128)(2,1)} %param.8, f32[4,512]{1,0:T(4,128)S(1)} %add_rsqrt_fusion), kind=kLoop, calls=%fused_computation.37 | loop fusion | flops 4718592 | bytes 6299648 | tf_op jit(solution)/shard_map/convert_element_type | solution.py:12
  13.5 0.2 dynamic-slice_reduce_fusion
  13.7 2.2 %fusion.48 = bf16[4,64,8,768]{3,2,1,0:T(8,128)(2,1)} fusion(f32[4,512]{1,0:T(4,128)S(1)} %add_rsqrt_fusion, bf16[4,512,768]{2,1,0:T(8,128)(2,1)S(1)} %copy-done.1), kind=kLoop, calls=%fused_computation.135 | loop fusion | flops 4718592 | bytes 6299648 | tf_op jit(solution)/shard_map/reshape | solution.py:51
  16.0 3.5 %gather_fusion.3 = bf16[64,8,768]{2,1,0:T(8,128)(2,1)} fusion(bf16[4,64,8,768]{3,2,1,0:T(8,128)(2,1)} %fusion.48, s32[64]{0:T(128)S(1)} %fusion.42), kind=kCustom, calls=%fused_computation.3 | custom fusion | bytes 1573376 | tf_op jit(solution)/shard_map/gather | solution.py:66
  19.4 13.1 %all-to-all-start.2 = ((bf16[64,8,768]{2,1,0:T(8,128)(2,1)}), bf16[64,8,768]{2,1,0:T(8,128)(2,1)S(1)}, u32[]{:S(2)}, u32[]{:S(2)}) async-start(bf16[64,8,768]{2,1,0:T(8,128)(2,1)} %gather_fusion.3), calls=%async_computation.2 | async-start | bytes 1572864 | tf_op jit(solution)/shard_map/all_to_all | solution.py:67
  32.9 0.8 gather_fusion.2
  33.7 0.2 dynamic-slice_reduce_fusion.1
  33.9 3.7 %gather_fusion.1 = bf16[64,8,768]{2,1,0:T(8,128)(2,1)} fusion(bf16[4,64,8,768]{3,2,1,0:T(8,128)(2,1)} %fusion.48, s32[64]{0:T(128)S(1)} %fusion.43), kind=kCustom, calls=%fused_computation.1 | custom fusion | bytes 1573376 | tf_op jit(solution)/shard_map/gather | solution.py:66
  37.7 0.8 gather_fusion
  38.8 0.1 broadcast_and_fusion.2
  39.0 0.1 broadcast_and_fusion.3
  39.2 16.4 %all-to-all-done.2 = bf16[64,8,768]{2,1,0:T(8,128)(2,1)S(1)} async-done(((bf16[64,8,768]{2,1,0:T(8,128)(2,1)}), bf16[64,8,768]{2,1,0:T(8,128)(2,1)S(1)}, u32[]{:S(2)}, u32[]{:S(2)}) %all-to-all-start.2) | async-done | bytes 786464 | tf_op jit(solution)/shard_map/all_to_all | solution.py:67
  55.6 5.9 %all-to-all-start = ((bf16[64,8,768]{2,1,0:T(8,128)(2,1)}), bf16[64,8,768]{2,1,0:T(8,128)(2,1)S(1)}, u32[]{:S(2)}, u32[]{:S(2)}) async-start(bf16[64,8,768]{2,1,0:T(8,128)(2,1)} %gather_fusion.1), calls=%async_computation | async-start | bytes 1572864 | tf_op jit(solution)/shard_map/all_to_all | solution.py:67
  61.5 76.8 %all-gather.2.cloned.1.call-done = bf16[4,2048,768]{2,1,0:T(8,128)(2,1)} async-done(((bf16[4,512,768]{2,1,0:T(8,128)(2,1)}), bf16[4,2048,768]{2,1,0:T(8,128)(2,1)}) %all-gather.2.cloned.1.call-update) | async-done | bytes 12582928 | tf_op jit(solution)/shard_map/all_gather | solution.py:52
  138.3 15.5 %while.27 = (s32[]{:T(128)}, f32[64,8]{1,0:T(8,128)}, f32[2,2,2048]{2,1,0:T(2,128)S(1)}, pred[2,64,2]{1,2,0:T(4,128)(4,1)S(1)}, pred[2,2,2048]{2,1,0:T(4,128)(4,...) while((s32[]{:T(128)}, f32[64,8]{1,0:T(8,128)}, ...), condition=%wide.region_11.12_spmd.clone, body=%wide.region_8.11_spmd.clone.sunk | while | flops 3229612544 | bytes 7160887 | solution.py:37
  138.8 6.2 %fusion.52 = (f32[2,2048]{1,0:T(2,128)S(1)}, f32[512]{0:T(512)S(1)}) fusion(pred[2,2048]{1,0:T(4,128)(4,1)S(1)} %dynamic-slice_bitcast_fusion.10, pred[512,2]{0,1:T(4,128)(4,1)S(1)} %broadcast_and_fusion.7, bf16[512,768]{1,0:T(8,128)(2,1)S(1)} %get-tuple-element.389, bf16[2,2,2048,768]{3,2,1,0:T(8,128)(2,1)} %get-tuple-element.388, s32[]{:T(128)S(6)} %copy.19), kind=kOutput, calls=%fused_computation.21.clone.1 | convolution fusion | flops 3229609472 | bytes 7101444 | tf_op jit(solution)/shard_map/while/body/eval_jaxpr/rd,cbd->rcb/dot_general | solution.py:30
  145.1 0.6 select_maximum_fusion.5
  146.2 6.2 %fusion.52 = (f32[2,2048]{1,0:T(2,128)S(1)}, f32[512]{0:T(512)S(1)}) fusion(pred[2,2048]{1,0:T(4,128)(4,1)S(1)} %dynamic-slice_bitcast_fusion.10, pred[512,2]{0,1:T(4,128)(4,1)S(1)} %broadcast_and_fusion.7, bf16[512,768]{1,0:T(8,128)(2,1)S(1)} %get-tuple-element.389, bf16[2,2,2048,768]{3,2,1,0:T(8,128)(2,1)} %get-tuple-element.388, s32[]{:T(128)S(6)} %copy.19), kind=kOutput, calls=%fused_computation.21.clone.1 | convolution fusion | flops 3229609472 | bytes 7101444 | tf_op jit(solution)/shard_map/while/body/eval_jaxpr/rd,cbd->rcb/dot_general | solution.py:30
  152.5 1.4 select_maximum_fusion.5
  153.9 10.9 %all-to-all-start.3 = ((f32[64,1,8]{2,1,0:T(1,128)}), f32[64,1,8]{2,1,0:T(1,128)S(1)}, u32[]{:S(2)}, u32[]{:S(2)}) async-start(f32[64,1,8]{2,1,0:T(1,128)} %bitcast.18), calls=%async_computation.3 | async-start | bytes 65536 | tf_op jit(solution)/shard_map/all_to_all | solution.py:74
  164.8 15.5 %while.26 = (s32[]{:T(128)}, f32[64,8]{1,0:T(8,128)}, f32[2,2,2048]{2,1,0:T(2,128)S(1)}, pred[2,64,2]{1,2,0:T(4,128)(4,1)S(1)}, pred[2,2,2048]{2,1,0:T(4,128)(4,...) while((s32[]{:T(128)}, f32[64,8]{1,0:T(8,128)}, ...), condition=%wide.region_5.6_spmd.clone, body=%wide.region_2.5_spmd.clone.sunk | while | flops 3229612544 | bytes 7160887 | solution.py:37
  165.2 6.2 %fusion.51 = (f32[2,2048]{1,0:T(2,128)S(1)}, f32[512]{0:T(512)S(1)}) fusion(pred[2,2048]{1,0:T(4,128)(4,1)S(1)} %dynamic-slice_bitcast_fusion.8, pred[512,2]{0,1:T(4,128)(4,1)S(1)} %broadcast_and_fusion.6, bf16[512,768]{1,0:T(8,128)(2,1)S(1)} %get-tuple-element.425, bf16[2,2,2048,768]{3,2,1,0:T(8,128)(2,1)} %get-tuple-element.424, s32[]{:T(128)S(6)} %copy.28), kind=kOutput, calls=%fused_computation.7.clone.1 | convolution fusion | flops 3229609472 | bytes 7101444 | tf_op jit(solution)/shard_map/while/body/eval_jaxpr/rd,cbd->rcb/dot_general | solution.py:30
  171.5 0.6 select_maximum_fusion.4
  172.6 6.2 %fusion.51 = (f32[2,2048]{1,0:T(2,128)S(1)}, f32[512]{0:T(512)S(1)}) fusion(pred[2,2048]{1,0:T(4,128)(4,1)S(1)} %dynamic-slice_bitcast_fusion.8, pred[512,2]{0,1:T(4,128)(4,1)S(1)} %broadcast_and_fusion.6, bf16[512,768]{1,0:T(8,128)(2,1)S(1)} %get-tuple-element.425, bf16[2,2,2048,768]{3,2,1,0:T(8,128)(2,1)} %get-tuple-element.424, s32[]{:T(128)S(6)} %copy.28), kind=kOutput, calls=%fused_computation.7.clone.1 | convolution fusion | flops 3229609472 | bytes 7101444 | tf_op jit(solution)/shard_map/while/body/eval_jaxpr/rd,cbd->rcb/dot_general | solution.py:30
  178.9 1.4 select_maximum_fusion.4
  180.4 12.3 %pmax.7 = f32[4,2048]{1,0:T(4,128)S(1)} all-reduce(f32[4,2048]{1,0:T(4,128)S(1)} %max.26), channel_id=1, replica_groups=mesh['gx'=64,'gy'=4] {'gy'}, use_global_device_ids=true, to_apply=%region_13.14 | all-reduce | flops 8192 | bytes 65536 | tf_op jit(solution)/shard_map/pmax | solution.py:83
  192.7 14.1 %all-to-all-start.1 = ((f32[64,1,8]{2,1,0:T(1,128)}), f32[64,1,8]{2,1,0:T(1,128)S(1)}, u32[]{:S(2)}, u32[]{:S(2)}) async-start(f32[64,1,8]{2,1,0:T(1,128)} %bitcast.9), calls=%async_computation.1 | async-start | bytes 65536 | tf_op jit(solution)/shard_map/all_to_all | solution.py:74
  206.8 0.2 select_reduce_fusion
  207.0 9.2 %all-to-all-done.1 = f32[64,1,8]{2,1,0:T(1,128)S(1)} async-done(((f32[64,1,8]{2,1,0:T(1,128)}), f32[64,1,8]{2,1,0:T(1,128)S(1)}, u32[]{:S(2)}, u32[]{:S(2)}) %all-to-all-start.1) | async-done | bytes 2080 | tf_op jit(solution)/shard_map/all_to_all | solution.py:74
  216.2 0.2 select_reduce_fusion.1
  216.6 0.7 maximum_select_fusion
  (82 shorter events, 3.1 us)
Async XLA Ops:
  6.5 7.2 %copy-start.1 = (bf16[4,512,768]{2,1,0:T(8,128)(2,1)S(1)}, bf16[4,512,768]{2,1,0:T(8,128)(2,1)}, u32[]{:S(2)}) copy-start(bf16[4,512,768]{2,1,0:T(8,128)(2,1)} %param.8) | copy-start | bytes 9437188
  6.5 6.9 %copy-start.3 = (s32[2,64,64]{2,1,0:T(8,128)S(1)}, s32[2,64,64]{2,1,0:T(8,128)}, u32[]{:S(2)}) copy-start(s32[2,64,64]{2,1,0:T(8,128)} %param.9) | copy-start | bytes 98308
  6.5 131.8 %all-gather.2.cloned.1.call-start = ((), (), s32[]{:S(2)}) async-start(), calls=%async_computation.4 | async-start | bytes 15728640 | tf_op jit(solution)/shard_map/all_gather | solution.py:52
  13.4 19.2 %copy-start.2 = (s32[2,64,64,2]{2,3,1,0:T(2,128)S(1)}, s32[2,64,64,2]{2,3,1,0:T(2,128)}, u32[]{:S(2)}) copy-start(s32[2,64,64,2]{2,3,1,0:T(2,128)} %param.10) | copy-start | bytes 196612
  13.4 19.2 %copy-start = (s32[256]{0:T(256)S(1)}, s32[256]{0:T(256)}, u32[]{:S(2)}) copy-start(s32[256]{0:T(256)} %param.11) | copy-start | bytes 3076
  19.4 36.2 %all-to-all-start.2 = ((bf16[64,8,768]{2,1,0:T(8,128)(2,1)}), bf16[64,8,768]{2,1,0:T(8,128)(2,1)S(1)}, u32[]{:S(2)}, u32[]{:S(2)}) async-start(bf16[64,8,768]{2,1,0:T(8,128)(2,1)} %gather_fusion.3), calls=%async_computation.2 | async-start | bytes 1572864 | tf_op jit(solution)/shard_map/all_to_all | solution.py:67
  55.6 98.3 %all-to-all-start = ((bf16[64,8,768]{2,1,0:T(8,128)(2,1)}), bf16[64,8,768]{2,1,0:T(8,128)(2,1)S(1)}, u32[]{:S(2)}, u32[]{:S(2)}) async-start(bf16[64,8,768]{2,1,0:T(8,128)(2,1)} %gather_fusion.1), calls=%async_computation | async-start | bytes 1572864 | tf_op jit(solution)/shard_map/all_to_all | solution.py:67
  153.9 38.8 %all-to-all-start.3 = ((f32[64,1,8]{2,1,0:T(1,128)}), f32[64,1,8]{2,1,0:T(1,128)S(1)}, u32[]{:S(2)}, u32[]{:S(2)}) async-start(f32[64,1,8]{2,1,0:T(1,128)} %bitcast.18), calls=%async_computation.3 | async-start | bytes 65536 | tf_op jit(solution)/shard_map/all_to_all | solution.py:74
  192.7 23.5 %all-to-all-start.1 = ((f32[64,1,8]{2,1,0:T(1,128)}), f32[64,1,8]{2,1,0:T(1,128)S(1)}, u32[]{:S(2)}, u32[]{:S(2)}) async-start(f32[64,1,8]{2,1,0:T(1,128)} %bitcast.9), calls=%async_computation.1 | async-start | bytes 65536 | tf_op jit(solution)/shard_map/all_to_all | solution.py:74
Sparse Core Ops, SparseCore 0:
  13.6 124.6 all-gather.1
where the time goes:
time: 225 us; the launch traced here: 224 us
  waiting for transfers between devices  102 us (45%)
  starting transfers between devices  44 us (20%)
  matrix products  24.8 us (11%)
  other arithmetic  15.5 us (7%)
  between operations  13.7 us (6%)
  blocking collectives  12.3 us (5%)
  local copies, waits for them, and re-layouts  11.2 us (5%)
    all_gather x1, waiting for transfers between devices, on_device(): owned_full = lax.all_gather(own_unit, 'gy', axis=1, tiled=True)  76.8 us
    all_to_all x2, starting transfers between devices, on_device(): lax.all_to_all(row_best, 'gx', split_axis=0, concat_axis=0, tiled=True)  24.9 us
    dot_general x4, matrix products, advance(): jnp.einsum('rd,cbd->rcb', flat_rows, columns, preferred_element_type=jnp....  24.8 us
    all_to_all x2, starting transfers between devices, on_device(): lax.all_to_all(outbound, 'gx', split_axis=0, concat_axis=0, tiled=True)  19.1 us
    all_to_all x2, waiting for transfers between devices, on_device(): lax.all_to_all(outbound, 'gx', split_axis=0, concat_axis=0, tiled=True)  16.4 us
    pmax x1, blocking collectives, on_device(): col_all = lax.pmax(col_total, 'gy')  12.3 us
    all_to_all x2, waiting for transfers between devices, on_device(): lax.all_to_all(row_best, 'gx', split_axis=0, concat_axis=0, tiled=True)  9.17 us
    gather x2, local copies, waits for them, and re-layouts, on_device(): outbound = own_pieces[outgoing_sent_block, outgoing_sent_piece]  7.19 us
  transfers between devices with their start and end apart: 5, of which 3 were waited for; matrix products, arithmetic and copies ran while one was open for 19% of the time, Pallas kernels for 0%

commit v1 on v0

--- a/solution.py
+++ b/solution.py
@@ -5,6 +5,14 @@
 
 SLICE = 8
 EPS = 1e-06
+
+
+def test_matrix(frame, array_axis):
+    frame = jnp.moveaxis(frame, 0, array_axis)
+    w1 = frame.shape
+    return frame.reshape(
+        *w1[:array_axis], w1[array_axis] * w1[array_axis + 1], *w1[array_axis + 2 :]
+    )
 
 
 def normalize(source):
@@ -39,6 +47,32 @@
 
 
 def on_device(embeds, fetch_list, partners, counts):
+
+    def _form_domain(my_tile, mesh_dim, d_out):
+        n = lax.psum(1, axis_name=mesh_dim)
+        nodes = [(k0, (k0 + 1) % n) for k0 in range(n)]
+        pages = [(q, j) for j, q in nodes]
+        e_now, found_now = ([], [])
+        p = 0
+        while p < n - 1:
+            if p % 2 == 0:
+                lower = lax.ppermute(
+                    e_now[-1] if e_now else my_tile, perm=nodes, axis_name=mesh_dim
+                )
+                e_now.append(lower)
+            else:
+                t1 = lax.ppermute(
+                    found_now[-1] if found_now else my_tile, axis_name=mesh_dim, perm=pages
+                )
+                found_now.append(t1)
+            p = p + 1
+        mixed_arr = jnp.stack([*e_now[::-1], my_tile, *found_now], axis=0)
+        res = lax.axis_index(mesh_dim)
+        q_next = len(e_now)
+        later = res - q_next
+        mixed_arr = mixed_arr[(jnp.arange(n) - later) % n]
+        return test_matrix(mixed_arr, d_out)
+
     owned, quarter, width = embeds.shape
     slice_rows = SLICE
     pieces = quarter // slice_rows
@@ -49,7 +83,7 @@
     waves = fetch_list.shape[0]
     own_unit = normalize(embeds)
     own_pieces = own_unit.reshape(owned, pieces, slice_rows, width)
-    owned_full = lax.all_gather(own_unit, "gy", axis=1, tiled=True)
+    owned_full = _form_domain(own_unit, "gy", 1)
     positions = jnp.arange(block, dtype=jnp.int32)
     own_counts = lax.dynamic_slice_in_dim(counts, first, owned)
     col_valid = positions[None, :] < own_counts[:, None]

time: 225 us -> 280 us (1.24)
  local copies, waits for them, and re-layouts: 11.2 us -> 36.3 us
  waiting for transfers between devices: 102 us -> 121 us
  other arithmetic: 15.5 us -> 29.6 us
  between operations: 13.7 us -> 0.33 us
  starting transfers between devices: 44 us -> 54.4 us
    ppermute x0 -> x3, waiting for transfers between devices: none -> 105 us  [the longest x2 105 us: _form_domain(): lax.ppermute(e_now[-1] if e_now else my_tile, perm=nodes, axis_name=mesh_...]
    all_gather x1 -> x0, waiting for transfers between devices: 76.8 us -> none  [on_device(): owned_full = lax.all_gather(own_unit, 'gy', axis=1, tiled=True)]
    gather x0 -> x3, local copies, waits for them, and re-layouts: none -> 19.4 us  [_form_domain(): mixed_arr = mixed_arr[(jnp.arange(n) - later) % n]]
    all_to_all x2, starting transfers between devices: 19.1 us -> 29.8 us  [on_device(): lax.all_to_all(outbound, 'gx', split_axis=0, concat_axis=0, tiled=True)]
    all_to_all x2, waiting for transfers between devices: 16.4 us -> 7.06 us  [on_device(): lax.all_to_all(outbound, 'gx', split_axis=0, concat_axis=0, tiled=True)]
    another operation x0 -> x2, other arithmetic: none -> 6.23 us  [_form_domain(): mixed_arr = jnp.stack([*e_now[::-1], my_tile, *found_now], axis=0)]
    transpose x0 -> x1, other arithmetic: none -> 6.19 us  [test_matrix(): frame = jnp.moveaxis(frame, 0, array_axis)]
    all_to_all x2, starting transfers between devices: 24.9 us -> 19.3 us  [on_device(): lax.all_to_all(row_best, 'gx', split_axis=0, concat_axis=0, tiled=True)]
  transfers between devices with their start and end apart: 5 -> 7, of which waited for: 3 -> 4; matrix products, arithmetic and copies ran while one was open for 19% -> 24% of each run, Pallas kernels for 0% -> 0%
where the time goes in v1:
time: 280 us; the launch traced here: 279 us
  waiting for transfers between devices  121 us (43%)
  starting transfers between devices  54.4 us (19%)
  local copies, waits for them, and re-layouts  36.3 us (13%)
  other arithmetic  29.6 us (11%)
  matrix products  25.2 us (9%)
  blocking collectives  11.6 us (4%)
    ppermute x2, waiting for transfers between devices, _form_domain(): lax.ppermute(e_now[-1] if e_now else my_tile, perm=nodes, axis_name=mesh_...  105 us
    all_to_all x2, starting transfers between devices, on_device(): lax.all_to_all(outbound, 'gx', split_axis=0, concat_axis=0, tiled=True)  29.8 us
    dot_general x4, matrix products, advance(): jnp.einsum('rd,cbd->rcb', flat_rows, columns, preferred_element_type=jnp....  25.2 us
    gather x3, local copies, waits for them, and re-layouts, _form_domain(): mixed_arr = mixed_arr[(jnp.arange(n) - later) % n]  19.4 us
    all_to_all x2, starting transfers between devices, on_device(): lax.all_to_all(row_best, 'gx', split_axis=0, concat_axis=0, tiled=True)  19.3 us
    pmax x1, blocking collectives, on_device(): col_all = lax.pmax(col_total, 'gy')  11.6 us
    all_to_all x2, waiting for transfers between devices, on_device(): lax.all_to_all(row_best, 'gx', split_axis=0, concat_axis=0, tiled=True)  9.16 us
    all_to_all x2, waiting for transfers between devices, on_device(): lax.all_to_all(outbound, 'gx', split_axis=0, concat_axis=0, tiled=True)  7.06 us
  transfers between devices with their start and end apart: 7, of which 4 were waited for; matrix products, arithmetic and copies ran while one was open for 24% of the time, Pallas kernels for 0%

profile of v1, /device:TPU:1, one launch (start us, length us, event | category | flops | bytes accessed | tf_op | source)
XLA Modules:
  0.0 278.8 jit_solution(9657387062562303953)
XLA Ops:
  0.0 2.7 fusion.18
  2.8 4.1 %fusion.19 = bf16[4,512,768]{2,1,0:T(8,128)(2,1)} fusion(bf16[4,512,768]{2,1,0:T(8,128)(2,1)} %param.8, f32[4,512]{1,0:T(4,128)S(1)} %add_rsqrt_fusion), kind=kLoop, calls=%fused_computation.41 | loop fusion | flops 4718592 | bytes 6299648 | tf_op jit(solution)/shard_map/convert_element_type | solution.py:20
  6.9 2.0 collective-permute-start
  8.9 1.3 collective-permute-start.2
  10.5 2.2 fusion.51
  12.7 3.5 %gather_fusion.1 = bf16[64,8,768]{2,1,0:T(8,128)(2,1)} fusion(bf16[4,64,8,768]{3,2,1,0:T(8,128)(2,1)} %fusion.51, s32[64]{0:T(128)S(1)} %fusion.45), kind=kCustom, calls=%fused_computation.1 | custom fusion | bytes 1573376 | tf_op jit(solution)/shard_map/gather | solution.py:100
  16.2 13.2 %all-to-all-start = ((bf16[64,8,768]{2,1,0:T(8,128)(2,1)}), bf16[64,8,768]{2,1,0:T(8,128)(2,1)}, u32[]{:S(2)}, u32[]{:S(2)}) async-start(bf16[64,8,768]{2,1,0:T(8,128)(2,1)} %gather_fusion.1), calls=%async_computation | async-start | bytes 1572864 | tf_op jit(solution)/shard_map/all_to_all | solution.py:101
  30.1 0.8 gather_fusion
  31.1 3.5 %gather_fusion.3 = bf16[64,8,768]{2,1,0:T(8,128)(2,1)} fusion(bf16[4,64,8,768]{3,2,1,0:T(8,128)(2,1)} %fusion.51, s32[64]{0:T(128)S(1)} %fusion.44), kind=kCustom, calls=%fused_computation.3 | custom fusion | bytes 1573376 | tf_op jit(solution)/shard_map/gather | solution.py:100
  34.6 41.5 %collective-permute-done = bf16[4,512,768]{2,1,0:T(8,128)(2,1)} collective-permute-done((bf16[4,512,768]{2,1,0:T(8,128)(2,1)}, bf16[4,512,768]{2,1,0:T(8,128)(2,1)}, u32[]{:S(2)}, u32[]{:S(2)}) %collective-permute-start) | collective-permute-done | bytes 3145760 | tf_op jit(solution)/shard_map/ppermute | solution.py:59
  76.1 1.9 collective-permute-start.1
  82.0 63.3 %collective-permute-done.1 = bf16[4,512,768]{2,1,0:T(8,128)(2,1)} collective-permute-done((bf16[4,512,768]{2,1,0:T(8,128)(2,1)}, bf16[4,512,768]{2,1,0:T(8,128)(2,1)}, u32[]{:S(2)}, u32[]{:S(2)}) %collective-permute-start.1) | collective-permute-done | bytes 3145760 | tf_op jit(solution)/shard_map/ppermute | solution.py:59
  145.3 5.7 %pad_maximum_fusion = bf16[4,4,512,768]{3,2,1,0:T(8,128)(2,1)S(1)} fusion(bf16[1,4,512,768]{3,2,1,0:T(8,128)(2,1)} %bitcast.5, bf16[1,4,512,768]{3,2,1,0:T(8,128)(2,1)S(1)} %fusion.52, bf16[1,4,512,768]{3,2,1,0:T(8,128)(2,1)} %bitcast.3, bf16[1,4,512,768]{3,2,1,0:T(8,128)(2,1)} %bitcast.2), kind=kLoop, calls=%fused_computation.36 | loop fusion | flops 18874368 | bytes 25165824 | tf_op jit(solution)/shard_map/stack | solution.py:69
  150.9 5.6 %fusion.48 = (bf16[4,4,512,384]{3,2,1,0:T(8,128)(2,1)}, bf16[4,4,512,384]{3,2,1,0:T(8,128)(2,1)}) fusion(bf16[4,4,512,768]{3,2,1,0:T(8,128)(2,1)S(1)} %pad_maximum_fusion), kind=kLoop, calls=%fused_computation.144 | loop fusion | bytes 25165824 | tf_op jit(solution)/shard_map/gather | solution.py:73
  156.6 6.9 %gather_fusion.4 = bf16[4,4,512,384]{3,2,1,0:T(8,128)(2,1)} fusion(bf16[4,4,512,384]{3,2,1,0:T(8,128)(2,1)} %get-tuple-element.215, s32[1024]{0:T(1024)S(1)} %pad_clamp_fusion.2), kind=kCustom, calls=%fused_computation.4 | custom fusion | bytes 12582928 | tf_op jit(solution)/shard_map/gather | solution.py:73
  163.4 6.8 %gather_fusion.5 = bf16[4,4,512,384]{3,2,1,0:T(8,128)(2,1)} fusion(bf16[4,4,512,384]{3,2,1,0:T(8,128)(2,1)} %get-tuple-element.216, s32[1024]{0:T(1024)S(1)} %pad_clamp_fusion.2), kind=kCustom, calls=%fused_computation.5 | custom fusion | bytes 12582928 | tf_op jit(solution)/shard_map/gather | solution.py:73
  170.3 6.2 %maximum_bitcast_fusion = bf16[4,4,512,768]{3,2,0,1:T(8,128)(2,1)S(1)} fusion(bf16[4,4,512,384]{3,2,1,0:T(8,128)(2,1)} %gather_fusion.5, bf16[4,4,512,384]{3,2,1,0:T(8,128)(2,1)} %gather_fusion.4), kind=kLoop, calls=%fused_computation.37 | loop fusion | flops 25165824 | bytes 25165824 | tf_op jit(solution)/shard_map/transpose | solution.py:11
  176.5 5.5 %copy.16 = bf16[4,4,512,768]{3,2,1,0:T(8,128)(2,1)} copy(bf16[4,4,512,768]{3,2,0,1:T(8,128)(2,1)S(1)} %maximum_bitcast_fusion) | data formatting | bytes 25165824 | tf_op jit(solution)/shard_map/transpose | solution.py:11
  182.0 16.7 %all-to-all-start.2 = ((bf16[64,8,768]{2,1,0:T(8,128)(2,1)}), bf16[64,8,768]{2,1,0:T(8,128)(2,1)S(1)}, u32[]{:S(2)}, u32[]{:S(2)}) async-start(bf16[64,8,768]{2,1,0:T(8,128)(2,1)} %gather_fusion.3), calls=%async_computation.2 | async-start | bytes 1572864 | tf_op jit(solution)/shard_map/all_to_all | solution.py:101
  198.7 15.9 %while.26 = (s32[]{:T(128)}, f32[64,8]{1,0:T(8,128)}, f32[2,2,2048]{2,1,0:T(2,128)S(1)}, pred[2,64,2]{1,2,0:T(4,128)(4,1)S(1)}, pred[2,2,2048]{2,1,0:T(4,128)(4,...) while((s32[]{:T(128)}, f32[64,8]{1,0:T(8,128)}, ...), condition=%wide.region_5.6_spmd.clone, body=%wide.region_2.5_spmd.clone.sunk | while | flops 3229612544 | bytes 7161387 | solution.py:45
  199.2 6.4 %fusion.55 = (f32[2,2048]{1,0:T(2,128)S(1)}, f32[512]{0:T(512)S(1)}) fusion(pred[2,2048]{1,0:T(4,128)(4,1)S(1)} %dynamic-slice_bitcast_fusion.8, pred[512,2]{0,1:T(4,128)(4,1)S(1)} %broadcast_and_fusion.6, bf16[512,768]{1,0:T(8,128)(2,1)} %get-tuple-element.427, bf16[2,2,2048,768]{3,2,1,0:T(8,128)(2,1)} %get-tuple-element.426, s32[]{:T(128)} %get-tuple-element.409), kind=kOutput, calls=%fused_computation.9.clone.1 | convolution fusion | flops 3229609472 | bytes 7101952 | tf_op jit(solution)/shard_map/while/body/eval_jaxpr/rd,cbd->rcb/dot_general | solution.py:38
  206.7 6.4 %fusion.55 = (f32[2,2048]{1,0:T(2,128)S(1)}, f32[512]{0:T(512)S(1)}) fusion(pred[2,2048]{1,0:T(4,128)(4,1)S(1)} %dynamic-slice_bitcast_fusion.8, pred[512,2]{0,1:T(4,128)(4,1)S(1)} %broadcast_and_fusion.6, bf16[512,768]{1,0:T(8,128)(2,1)} %get-tuple-element.427, bf16[2,2,2048,768]{3,2,1,0:T(8,128)(2,1)} %get-tuple-element.426, s32[]{:T(128)} %get-tuple-element.409), kind=kOutput, calls=%fused_computation.9.clone.1 | convolution fusion | flops 3229609472 | bytes 7101952 | tf_op jit(solution)/shard_map/while/body/eval_jaxpr/rd,cbd->rcb/dot_general | solution.py:38
  213.2 1.4 select_maximum_fusion.4
  214.6 7.1 %all-to-all-done.2 = bf16[64,8,768]{2,1,0:T(8,128)(2,1)S(1)} async-done(((bf16[64,8,768]{2,1,0:T(8,128)(2,1)}), bf16[64,8,768]{2,1,0:T(8,128)(2,1)S(1)}, u32[]{:S(2)}, u32[]{:S(2)}) %all-to-all-start.2) | async-done | bytes 786464 | tf_op jit(solution)/shard_map/all_to_all | solution.py:101
  221.7 15.5 %while.27 = (s32[]{:T(128)}, f32[64,8]{1,0:T(8,128)}, f32[2,2,2048]{2,1,0:T(2,128)S(1)}, pred[2,64,2]{1,2,0:T(4,128)(4,1)S(1)}, pred[2,2,2048]{2,1,0:T(4,128)(4,...) while((s32[]{:T(128)}, f32[64,8]{1,0:T(8,128)}, ...), condition=%wide.region_11.12_spmd.clone, body=%wide.region_8.11_spmd.clone.sunk | while | flops 3229612544 | bytes 7161387 | solution.py:45
  222.2 6.2 %fusion.56 = (f32[2,2048]{1,0:T(2,128)S(1)}, f32[512]{0:T(512)S(1)}) fusion(pred[2,2048]{1,0:T(4,128)(4,1)S(1)} %dynamic-slice_bitcast_fusion.10, pred[512,2]{0,1:T(4,128)(4,1)S(1)} %broadcast_and_fusion.7, bf16[512,768]{1,0:T(8,128)(2,1)S(1)} %get-tuple-element.391, bf16[2,2,2048,768]{3,2,1,0:T(8,128)(2,1)} %get-tuple-element.390, ...), kind=kOutput, calls=%fused_computation.23.clone.1 | convolution fusion | flops 3229609472 | bytes 7101952 | tf_op jit(solution)/shard_map/while/body/eval_jaxpr/rd,cbd->rcb/dot_general | solution.py:38
  229.6 6.2 %fusion.56 = (f32[2,2048]{1,0:T(2,128)S(1)}, f32[512]{0:T(512)S(1)}) fusion(pred[2,2048]{1,0:T(4,128)(4,1)S(1)} %dynamic-slice_bitcast_fusion.10, pred[512,2]{0,1:T(4,128)(4,1)S(1)} %broadcast_and_fusion.7, bf16[512,768]{1,0:T(8,128)(2,1)S(1)} %get-tuple-element.391, bf16[2,2,2048,768]{3,2,1,0:T(8,128)(2,1)} %get-tuple-element.390, ...), kind=kOutput, calls=%fused_computation.23.clone.1 | convolution fusion | flops 3229609472 | bytes 7101952 | tf_op jit(solution)/shard_map/while/body/eval_jaxpr/rd,cbd->rcb/dot_general | solution.py:38
  235.9 1.4 select_maximum_fusion.5
  237.3 5.9 %all-to-all-start.1 = ((f32[64,1,8]{2,1,0:T(1,128)}), f32[64,1,8]{2,1,0:T(1,128)S(1)}, u32[]{:S(2)}, u32[]{:S(2)}) async-start(f32[64,1,8]{2,1,0:T(1,128)} %bitcast.15), calls=%async_computation.1 | async-start | bytes 65536 | tf_op jit(solution)/shard_map/all_to_all | solution.py:108
  243.2 11.6 %pmax.7 = f32[4,2048]{1,0:T(4,128)S(1)} all-reduce(f32[4,2048]{1,0:T(4,128)S(1)} %max.26), channel_id=1, replica_groups=mesh['gx'=64,'gy'=4] {'gy'}, use_global_device_ids=true, to_apply=%region_13.14 | all-reduce | flops 8192 | bytes 65536 | tf_op jit(solution)/shard_map/pmax | solution.py:117
  254.8 13.4 %all-to-all-start.3 = ((f32[64,1,8]{2,1,0:T(1,128)}), f32[64,1,8]{2,1,0:T(1,128)S(1)}, u32[]{:S(2)}, u32[]{:S(2)}) async-start(f32[64,1,8]{2,1,0:T(1,128)} %bitcast.24), calls=%async_computation.3 | async-start | bytes 65536 | tf_op jit(solution)/shard_map/all_to_all | solution.py:108
  268.5 9.2 %all-to-all-done.3 = f32[64,1,8]{2,1,0:T(1,128)S(1)} async-done(((f32[64,1,8]{2,1,0:T(1,128)}), f32[64,1,8]{2,1,0:T(1,128)S(1)}, u32[]{:S(2)}, u32[]{:S(2)}) %all-to-all-start.3) | async-done | bytes 2080 | tf_op jit(solution)/shard_map/all_to_all | solution.py:108
  (104 shorter events, 9.7 us)
Async XLA Ops:
  0.0 10.5 %copy-start.1 = (bf16[4,512,768]{2,1,0:T(8,128)(2,1)S(1)}, bf16[4,512,768]{2,1,0:T(8,128)(2,1)}, u32[]{:S(2)}) copy-start(bf16[4,512,768]{2,1,0:T(8,128)(2,1)} %param.8) | copy-start | bytes 9437188
  0.0 10.3 %copy-start.5 = (s32[2,64,64]{2,1,0:T(8,128)S(1)}, s32[2,64,64]{2,1,0:T(8,128)}, u32[]{:S(2)}) copy-start(s32[2,64,64]{2,1,0:T(8,128)} %param.9) | copy-start | bytes 98308
  6.9 22.5 %copy-start = (s32[256]{0:T(256)S(1)}, s32[256]{0:T(256)}, u32[]{:S(2)}) copy-start(s32[256]{0:T(256)} %param.11) | copy-start | bytes 3076
  6.9 22.7 %copy-start.2 = (s32[2,64,64,2]{2,3,1,0:T(2,128)S(1)}, s32[2,64,64,2]{2,3,1,0:T(2,128)}, u32[]{:S(2)}) copy-start(s32[2,64,64,2]{2,3,1,0:T(2,128)} %param.10) | copy-start | bytes 196612
  6.9 69.2 %collective-permute-start = (bf16[4,512,768]{2,1,0:T(8,128)(2,1)}, bf16[4,512,768]{2,1,0:T(8,128)(2,1)}, u32[]{:S(2)}, u32[]{:S(2)}) collective-permute-start(bf16[4,512,768]{2,1,0:T(8,128)(2,1)} %fusion.19), channel_id=1, source_target_pairs={{0,1},{1,2},{2,3},{3,0},{4,5},{5,6},{6,7},{7,4},{8,9},{9,10},{10,1... | collective-permute-start | bytes 9437192 | tf_op jit(solution)/shard_map/ppermute | solution.py:59
  8.9 73.0 %collective-permute-start.2 = (bf16[4,512,768]{2,1,0:T(8,128)(2,1)}, bf16[4,512,768]{2,1,0:T(8,128)(2,1)}, u32[]{:S(2)}, u32[]{:S(2)}) collective-permute-start(bf16[4,512,768]{2,1,0:T(8,128)(2,1)} %fusion.19), channel_id=1, source_target_pairs={{1,0},{2,1},{3,2},{0,3},{5,4},{6,5},{7,6},{4,7},{9,8},{10,9},{11,1... | collective-permute-start | bytes 9437192 | tf_op jit(solution)/shard_map/ppermute | solution.py:64
  16.2 165.8 %all-to-all-start = ((bf16[64,8,768]{2,1,0:T(8,128)(2,1)}), bf16[64,8,768]{2,1,0:T(8,128)(2,1)}, u32[]{:S(2)}, u32[]{:S(2)}) async-start(bf16[64,8,768]{2,1,0:T(8,128)(2,1)} %gather_fusion.1), calls=%async_computation | async-start | bytes 1572864 | tf_op jit(solution)/shard_map/all_to_all | solution.py:101
  29.5 0.6 copy-start.7
  76.1 69.1 %collective-permute-start.1 = (bf16[4,512,768]{2,1,0:T(8,128)(2,1)}, bf16[4,512,768]{2,1,0:T(8,128)(2,1)}, u32[]{:S(2)}, u32[]{:S(2)}) collective-permute-start(bf16[4,512,768]{2,1,0:T(8,128)(2,1)} %collective-permute-done), channel_id=1, source_target_pairs={{0,1},{1,2},{2,3},{3,0},{4,5},{5,6},{6,7},{7,4},{8,9},{9,10},{10,1... | collective-permute-start | bytes 9437192 | tf_op jit(solution)/shard_map/ppermute | solution.py:59
  182.0 39.7 %all-to-all-start.2 = ((bf16[64,8,768]{2,1,0:T(8,128)(2,1)}), bf16[64,8,768]{2,1,0:T(8,128)(2,1)S(1)}, u32[]{:S(2)}, u32[]{:S(2)}) async-start(bf16[64,8,768]{2,1,0:T(8,128)(2,1)} %gather_fusion.3), calls=%async_computation.2 | async-start | bytes 1572864 | tf_op jit(solution)/shard_map/all_to_all | solution.py:101
  221.7 46.5 %copy-start.4 = (pred[64,4,64]{2,1,0:T(4,128)(4,1)S(1)}, pred[64,4,64]{2,1,0:T(4,128)(4,1)}, u32[]{:S(2)}) copy-start(pred[64,4,64]{2,1,0:T(4,128)(4,1)} %broadcast_and_fusion.3) | copy-start | bytes 49156
  221.7 55.9 %copy-start.3 = (pred[64,4,64]{2,1,0:T(4,128)(4,1)S(1)}, pred[64,4,64]{2,1,0:T(4,128)(4,1)}, u32[]{:S(2)}) copy-start(pred[64,4,64]{2,1,0:T(4,128)(4,1)} %broadcast_and_fusion.2) | copy-start | bytes 49156
  221.7 56.4 %copy-start.6 = (s32[512]{0:T(512)S(1)}, s32[512]{0:T(512)}, u32[]{:S(2)}) copy-start(s32[512]{0:T(512)} %iota_add_fusion) | copy-start | bytes 6148
  221.7 56.4 %copy-start.8 = (s32[4]{0:T(128)S(1)}, s32[4]{0:T(128)}, u32[]{:S(2)}) copy-start(s32[4]{0:T(128)} %copy-done.7) | copy-start | bytes 52
  237.3 17.5 %all-to-all-start.1 = ((f32[64,1,8]{2,1,0:T(1,128)}), f32[64,1,8]{2,1,0:T(1,128)S(1)}, u32[]{:S(2)}, u32[]{:S(2)}) async-start(f32[64,1,8]{2,1,0:T(1,128)} %bitcast.15), calls=%async_computation.1 | async-start | bytes 65536 | tf_op jit(solution)/shard_map/all_to_all | solution.py:108
  254.8 22.8 %all-to-all-start.3 = ((f32[64,1,8]{2,1,0:T(1,128)}), f32[64,1,8]{2,1,0:T(1,128)S(1)}, u32[]{:S(2)}, u32[]{:S(2)}) async-start(f32[64,1,8]{2,1,0:T(1,128)} %bitcast.24), calls=%async_computation.3 | async-start | bytes 65536 | tf_op jit(solution)/shard_map/all_to_all | solution.py:108
